TPU v7x, 512 devices: a whole 4x4x16 slice. The times are simulated.
512 devices in a mesh: ctx: 64 (over z_hi, y, x), ch: 8 (over z_lo, core).
Axes of the slice: x: 4, y: 4, z: 16 (z_hi: 4, z_lo: 4; z = z_hi * 4 + z_lo), core: 2. Of those that a mesh axis runs over, the one named last changes fastest.
Arguments:
- first_gate: bfloat16 [8192, 8192], P('ctx', 'ch'), may hold values from -6 to 6
- second_gate: bfloat16 [8192, 8192], P('ctx', 'ch'), may hold values from -6 to 6
- output_gate: bfloat16 [8192, 8192], P('ctx', 'ch'), may hold values from -6 to 6
- values: bfloat16 [8192, 8192], P('ctx', 'ch'), may hold values from -6 to 6
- cotangent: bfloat16 [8192, 8192], P('ctx', 'ch'), may hold values from -6 to 6
- medium_filter: bfloat16 [128, 512], P(None, 'ch'), may hold values from -0.5 to 0.5
- long_filter: bfloat16 [8192, 512], P('ctx', 'ch'), may hold values from -0.044194174 to 0.044194174
Outputs:
- grad_first: bfloat16 [8192, 8192], P('ctx', 'ch')
- grad_second: bfloat16 [8192, 8192], P('ctx', 'ch')
- grad_output_gate: bfloat16 [8192, 8192], P('ctx', 'ch')
- grad_values: bfloat16 [8192, 8192], P('ctx', 'ch')
- grad_medium: float32 [128, 512], P(None, 'ch')
- grad_long: bfloat16 [8192, 512], P('ctx', 'ch')
- filter_rms: float32 [], replicated
All inputs are finite; a program needn't handle non-finite values.
Results may differ from a plain program's by a relative error of at most 0.011.
Values may be sent and summed in bfloat16 or wider, within the bound.
No kernel may reach another device: no remote copies, remote signals or barrier semaphores. Data moves between devices by JAX's collectives and lax.ppermute only.
A program may use at most 64 MiB of HBM per device.

v0:
```python
import math
import jax
import jax.numpy as jnp
from jax import lax
from jax.sharding import PartitionSpec as P

radix_cols = 128
block_limit = 64
highest = lax.Precision.HIGH
wide_type = jnp.float32
narrow_type = jnp.bfloat16


def passed_along(array, axis, by):
    peers = lax.axis_size(axis)
    pairs = [(i, i + by) for i in range(peers) if 0 <= i + by < peers]
    return lax.ppermute(array, axis, pairs)


def band_table(filt, block_rows, flipped):
    tap_count, group_count = filt.shape
    window_rows = block_rows + tap_count - 1
    leading = filt[::-1] if flipped else filt
    padded = jnp.concatenate([leading.T, jnp.zeros((group_count, block_rows), filt.dtype)], axis=1)
    tiled = jnp.broadcast_to(padded[:, None, :], (group_count, block_rows, window_rows + 1))
    tiled = tiled.reshape(group_count, block_rows * (window_rows + 1))
    return tiled[:, : block_rows * window_rows].reshape(group_count, block_rows, window_rows)


def windows_of(extended, block_rows, block_count, window_rows):
    return jnp.stack(
        [
            extended[number * block_rows : number * block_rows + window_rows]
            for number in range(block_count)
        ]
    )


def phase_table(row_count, col_count, period):
    row_ids = lax.broadcasted_iota(jnp.int32, (row_count, col_count), 0)
    col_ids = lax.broadcasted_iota(jnp.int32, (row_count, col_count), 1)
    angle = (row_ids * col_ids % period).astype(wide_type) * (2.0 * math.pi / period)
    return (jnp.cos(angle), jnp.sin(angle))


def forward_dft(signal, tables):
    outer_table, cos_twist, sin_twist, forward_inner, inverse_inner = tables
    outer = jnp.einsum("kna,nmb->mkab", outer_table, signal, precision=highest)
    real_part = outer[:, 0]
    imag_part = outer[:, 1]
    twisted = jnp.stack(
        [
            real_part * cos_twist + imag_part * sin_twist,
            imag_part * cos_twist - real_part * sin_twist,
        ],
        axis=1,
    )
    return jnp.einsum("mkab,kjbq->mjaq", twisted, forward_inner, precision=highest)


def inverse_dft(spectrum, tables, total_len):
    outer_table, cos_twist, sin_twist, forward_inner, inverse_inner = tables
    inner = jnp.einsum("mkab,kjbq->mjaq", spectrum, inverse_inner, precision=highest)
    real_part = inner[:, 0]
    imag_part = inner[:, 1]
    twisted = jnp.stack(
        [
            real_part * cos_twist - imag_part * sin_twist,
            imag_part * cos_twist + real_part * sin_twist,
        ],
        axis=1,
    )
    signal = jnp.einsum("kna,mkab->nmb", outer_table, twisted, precision=highest)
    return signal / total_len


def split_wide(value):
    high = value.astype(narrow_type)
    low = (value - high.astype(wide_type)).astype(narrow_type)
    return (high, low)


def joined_wide(high, low):
    return high.astype(wide_type) + low.astype(wide_type)


def medium_bands(filt):
    tap_count, item_count = filt.shape
    bands = band_table(filt, tap_count, False)
    near = bands[:, :, :tap_count]
    far = jnp.concatenate(
        [bands[:, :, tap_count:], jnp.zeros((item_count, tap_count, 1), filt.dtype)], axis=2
    )
    return (near, far)


def channel_work(pieces, filt):
    gated_part, grad_part, gate_part, filter_part = pieces
    half_rows = gated_part.shape[0]
    chan_total = gated_part.shape[1]
    item_count = filter_part.shape[1]
    group_size = chan_total // item_count
    seq_len = half_rows * radix_cols
    full_rows = 2 * half_rows
    total_len = 2 * seq_len
    scale = 1.0 / math.sqrt(seq_len * group_size)
    by_item = (half_rows, item_count, group_size, radix_cols)
    near, far = medium_bands(filt)
    gated_items = gated_part.reshape(by_item)
    gated_prev = jnp.concatenate([jnp.zeros_like(gated_items[:1]), gated_items[:-1]], axis=0)
    mixed = (
        jnp.einsum("ngcs,gsr->ngcr", gated_items, near, preferred_element_type=wide_type)
        + jnp.einsum("ngcs,gsr->ngcr", gated_prev, far, preferred_element_type=wide_type)
    ).reshape(half_rows, chan_total, radix_cols)
    gate_wide = gate_part.astype(wide_type)
    carried = (gate_wide * mixed).astype(narrow_type)
    cos_outer, sin_outer = phase_table(half_rows, full_rows, full_rows)
    cos_twist, sin_twist = phase_table(full_rows, radix_cols, total_len)
    cos_inner, sin_inner = phase_table(radix_cols, radix_cols, radix_cols)
    outer_table = jnp.stack([cos_outer, -sin_outer])
    forward_inner = jnp.stack(
        [jnp.stack([cos_inner, -sin_inner]), jnp.stack([sin_inner, cos_inner])]
    )
    inverse_inner = jnp.stack(
        [jnp.stack([cos_inner, sin_inner]), jnp.stack([-sin_inner, cos_inner])]
    )
    tables = (outer_table, cos_twist, sin_twist, forward_inner, inverse_inner)
    shaped = (item_count, group_size, 2, full_rows, radix_cols)
    flat_shape = (chan_total, 2, full_rows, radix_cols)
    signals = jnp.concatenate([carried, grad_part], axis=1).astype(wide_type)
    both_specs = forward_dft(signals, tables)
    gated_spec = both_specs[:chan_total].reshape(shaped)
    inner_spec = both_specs[chan_total:].reshape(shaped)
    filt_spec = forward_dft(filter_part.astype(wide_type), tables)[:, None]
    gated_re = gated_spec[:, :, 0]
    gated_im = gated_spec[:, :, 1]
    inner_re = inner_spec[:, :, 0]
    inner_im = inner_spec[:, :, 1]
    filt_re = filt_spec[:, :, 0]
    filt_im = filt_spec[:, :, 1]
    conv_spec = jnp.stack(
        [gated_re * filt_re - gated_im * filt_im, gated_re * filt_im + gated_im * filt_re], axis=2
    )
    back_spec = jnp.stack(
        [inner_re * filt_re + inner_im * filt_im, inner_im * filt_re - inner_re * filt_im], axis=2
    )
    corr_spec = jnp.stack(
        [inner_re * gated_re + inner_im * gated_im, inner_im * gated_re - inner_re * gated_im],
        axis=2,
    )
    signals_back = inverse_dft(
        jnp.concatenate([conv_spec.reshape(flat_shape), back_spec.reshape(flat_shape)], axis=0),
        tables,
        total_len,
    )
    second_mix = signals_back[:, :chan_total].astype(narrow_type)
    grad_carried = signals_back[:, chan_total:].astype(narrow_type).astype(wide_type)
    summed = jnp.sum(corr_spec, axis=1)
    lagged = (inverse_dft(summed, tables, total_len) * scale).astype(narrow_type)
    grad_second = (grad_carried * mixed).astype(narrow_type)
    grad_mixed = (grad_carried * gate_wide).astype(narrow_type)
    mixed_items = grad_mixed.reshape(by_item)
    mixed_next = jnp.concatenate([mixed_items[1:], jnp.zeros_like(mixed_items[:1])], axis=0)
    grad_gated = (
        jnp.einsum("ngcs,grs->ngcr", mixed_items, near, preferred_element_type=wide_type)
        + jnp.einsum("ngcs,grs->ngcr", mixed_next, far, preferred_element_type=wide_type)
    ).reshape(half_rows, chan_total, radix_cols)
    tap_count = filt.shape[0]
    own_lags = jnp.einsum(
        "ngcs,ngcr->gsr", gated_items, mixed_items, preferred_element_type=wide_type
    )
    prev_lags = jnp.einsum(
        "ngcs,ngcr->gsr", gated_prev, mixed_items, preferred_element_type=wide_type
    )
    cube = (tap_count, tap_count, tap_count)
    lag_of = lax.broadcasted_iota(jnp.int32, cube, 2) - lax.broadcasted_iota(jnp.int32, cube, 1)
    lag_ids = lax.broadcasted_iota(jnp.int32, cube, 0)
    on_own = (lag_of == lag_ids)[None]
    on_prev = (lag_of + tap_count == lag_ids)[None]
    grad_medium = (
        jnp.sum(
            jnp.where(on_own, own_lags[:, None], 0.0) + jnp.where(on_prev, prev_lags[:, None], 0.0),
            axis=(2, 3),
        )
        * scale
    )
    squares = jnp.sum(jnp.square(lagged.astype(wide_type))) + jnp.sum(grad_medium * grad_medium)
    squares = lax.psum(squares, "ch")
    medium_high, medium_low = split_wide(grad_medium)
    squares_high, squares_low = split_wide(squares)
    squares_row = jnp.concatenate(
        [
            squares_high.reshape(1, 1),
            squares_low.reshape(1, 1),
            jnp.zeros((1, radix_cols - 2), narrow_type),
        ],
        axis=1,
    )
    shared = jnp.concatenate([medium_high, medium_low, squares_row], axis=0)
    shared = jnp.broadcast_to(shared[None], (half_rows,) + shared.shape)
    return jnp.concatenate(
        [second_mix, grad_second, grad_gated.astype(narrow_type), lagged, shared], axis=1
    )


def body(first_gate, second_gate, output_gate, values, cotangent, medium_filter, long_filter):
    tok_rows, chan_local = first_gate.shape
    tap_count, local_groups = medium_filter.shape
    group_size = chan_local // local_groups
    ctx_devices = lax.axis_size("ctx")
    ctx_groups = local_groups // ctx_devices
    chan_share = ctx_groups * group_size
    first_wide = first_gate.astype(wide_type)
    values_wide = values.astype(wide_type)
    cotangent_wide = cotangent.astype(wide_type)
    gated_input = (first_wide * values_wide).astype(narrow_type)
    grad_inner = (cotangent_wide * output_gate.astype(wide_type)).astype(narrow_type)

    def token_major(matrix):
        return matrix.T.reshape(ctx_devices, -1, tok_rows)

    outbound = jnp.concatenate(
        [
            token_major(gated_input),
            token_major(grad_inner),
            token_major(second_gate),
            token_major(long_filter),
        ],
        axis=1,
    )
    arrived = lax.all_to_all(outbound, "ctx", 0, 0, tiled=True)
    own_filter = lax.dynamic_slice_in_dim(
        medium_filter, lax.axis_index("ctx") * ctx_groups, ctx_groups, axis=1
    )
    returned = channel_work(
        (
            arrived[:, :chan_share],
            arrived[:, chan_share : 2 * chan_share],
            arrived[:, 2 * chan_share : 3 * chan_share],
            arrived[:, 3 * chan_share :],
        ),
        own_filter,
    )
    back = lax.all_to_all(returned, "ctx", 0, 0, tiled=True)

    def token_rows(start, count):
        return back[:, start : start + count].reshape(ctx_devices * count, tok_rows).T

    second_mix = token_rows(0, chan_share)
    grad_second = token_rows(chan_share, chan_share)
    grad_gated = token_rows(2 * chan_share, chan_share).astype(wide_type)
    grad_long = token_rows(3 * chan_share, ctx_groups)
    grad_medium = joined_wide(
        token_rows(3 * chan_share + ctx_groups, ctx_groups),
        token_rows(3 * chan_share + 2 * ctx_groups, ctx_groups),
    )
    squares_row = back[:, 3 * chan_share + 3 * ctx_groups]
    total_squares = jnp.sum(joined_wide(squares_row[:, 0], squares_row[:, 1]))
    grad_output_gate = (cotangent_wide * second_mix.astype(wide_type)).astype(narrow_type)
    grad_first = (grad_gated * values_wide).astype(narrow_type)
    grad_values = (grad_gated * first_wide).astype(narrow_type)
    entries = (tok_rows * ctx_devices + tap_count) * local_groups * lax.axis_size("ch")
    filter_rms = jnp.sqrt(total_squares / entries)
    return (
        grad_first,
        grad_second,
        grad_output_gate,
        grad_values,
        grad_medium,
        grad_long,
        filter_rms,
    )


def solution(mesh):
    return jax.shard_map(
        body,
        mesh=mesh,
        in_specs=(
            P("ctx", "ch"),
            P("ctx", "ch"),
            P("ctx", "ch"),
            P("ctx", "ch"),
            P("ctx", "ch"),
            P(None, "ch"),
            P("ctx", "ch"),
        ),
        out_specs=(
            P("ctx", "ch"),
            P("ctx", "ch"),
            P("ctx", "ch"),
            P("ctx", "ch"),
            P(None, "ch"),
            P("ctx", "ch"),
            P(),
        ),
        check_vma=False,
    )
```

profile of v0, /device:TPU:1, one launch (start us, length us, event | category | flops | bytes accessed | tf_op | source)
XLA Modules:
  0.0 178.5 jit_solution(15019823692535973274)
XLA Ops:
  0.7 1.2 copy.100
  1.8 1.1 copy.99
  3.0 1.1 copy.101
  4.1 1.1 copy.102
  5.6 1.0 pad_maximum_fusion
  6.6 21.7 %all-to-all-start = ((bf16[64,49,128]{2,1,0:T(8,128)(2,1)}), bf16[64,49,128]{2,1,0:T(8,128)(2,1)S(1)}, u32[]{:S(2)}, u32[]{:S(2)}) async-start(bf16[64,49,128]{2,1,0:T(8,128)(2,1)} %pad_maximum_fusion), calls=%async_computation | async-start | bytes 1835008 | tf_op jit(solution)/shard_map/all_to_all | solution.py:231
  28.5 0.4 slice_reduce_fusion
  28.9 0.3 reshape.489
  30.3 39.9 %all-to-all-done = bf16[64,49,128]{2,1,0:T(8,128)(2,1)S(1)} async-done(((bf16[64,49,128]{2,1,0:T(8,128)(2,1)}), bf16[64,49,128]{2,1,0:T(8,128)(2,1)S(1)}, u32[]{:S(2)}, u32[]{:S(2)}) %all-to-all-start) | async-done | bytes 802848 | tf_op jit(solution)/shard_map/all_to_all | solution.py:231
  70.9 1.3 convolution_bitcast_fusion
  72.2 0.8 multiply_add_fusion.1
  73.1 2.1 %fusion.12 = f32[32,2,128,128]{2,3,0,1:T(8,128)S(1)} fusion(f32[32,1,128,128]{2,3,1,0:T(8,128)S(1)} %get-tuple-element.38, f32[32,1,128,128]{2,3,1,0:T(8,128)S(1)} %get-tuple-element.37, f32[1,2,128,128]{2,3,0,1:T(8,128)S(1)} %get-tuple-element.64, f32[1,2,128,128]{2,3,0,1:T(8,128)S(1)} %get-tuple-element.71), kind=kOutput, calls=%fused_computation.16 | convolution fusion | flops 1611726848 | bytes 8650752 | tf_op jit(solution)/shard_map/mkab,kjbq->mjaq/dot_general | solution.py:58
  75.7 0.3 multiply_add_fusion.6
  76.0 0.3 convolution_bitcast_fusion.2
  76.3 1.2 multiply_add_fusion.2
  77.8 2.1 %fusion.9 = f32[32,2,128,128]{2,3,1,0:T(8,128)S(1)} fusion(f32[16,2,128,128]{2,3,0,1:T(8,128)S(1)} %maximum_bitcast_fusion.6, f32[16,2,128,128]{2,3,0,1:T(8,128)S(1)} %maximum_bitcast_fusion.5, f32[1,2,128,128]{2,3,1,0:T(8,128)S(1)} %get-tuple-element.72, f32[1,2,128,128]{2,3,1,0:T(8,128)S(1)} %get-tuple-element.63), kind=kOutput, calls=%fused_computation.15 | convolution fusion | flops 1611726848 | bytes 8650752 | tf_op jit(solution)/shard_map/mkab,kjbq->mjaq/dot_general | solution.py:63
  79.9 0.8 multiply_subtract_fusion
  80.7 2.2 %fusion.19 = bf16[64,32,128]{2,0,1:T(8,128)(2,1)S(1)} fusion(f32[32,1,128,128]{2,3,1,0:T(8,128)S(1)} %get-tuple-element.36, f32[32,1,128,128]{2,3,1,0:T(8,128)S(1)} %get-tuple-element.35, f32[1,64,128]{2,1,0:T(8,128)S(1)} %get-tuple-element.79, f32[1,64,128]{2,1,0:T(8,128)S(1)} %get-tuple-element.80), kind=kOutput, calls=%fused_computation.29 | convolution fusion | flops 404242432 | bytes 4784128 | tf_op jit(solution)/shard_map/kna,mkab->nmb/dot_general | solution.py:73
  83.9 2.5 %add_reduce_fusion = f32[128]{0:T(128)S(1)} fusion(f32[128,128]{1,0:T(8,128)S(1)} %convolution_bitcast_fusion.4, f32[128,128]{1,0:T(8,128)S(1)} %convolution_bitcast_fusion.5), kind=kLoop, calls=%fused_computation | loop fusion | flops 16777088 | bytes 131584 | tf_op jit(solution)/shard_map/reduce_sum | solution.py:181
  86.4 0.6 bitcast_convert_fusion
  87.4 0.3 multiply_subtract_fusion.5
  88.3 0.6 multiply_reduce_fusion
  90.2 21.0 %psum.7 = f32[]{:T(128)} all-reduce(f32[]{:T(128)S(6)} %add.226), channel_id=1, replica_groups=mesh['ctx'=64,'ch'=8] {'ch'}, use_global_device_ids=true, to_apply=%region_4.5 | all-reduce | flops 1 | bytes 8 | tf_op jit(solution)/shard_map/psum | solution.py:188
  112.6 0.6 copy.118
  113.2 57.7 %all_to_all.10 = bf16[64,52,128]{2,1,0:T(8,128)(2,1)S(1)} all-to-all(bf16[64,52,128]{2,1,0:T(8,128)(2,1)S(1)} %copy.118), channel_id=1, replica_groups=mesh['ctx'=64,'ch'=8] {'ctx'}, dimensions={0} | all-to-all | bytes 1703936 | tf_op jit(solution)/shard_map/all_to_all | solution.py:244
  171.2 0.8 copy.121
  172.0 0.8 copy.124
  173.0 0.8 copy.123
  173.8 0.8 copy.122
  174.7 0.7 add_reduce_fusion.1
  176.1 0.6 copy.173
  176.7 0.7 fusion.83
  (52 shorter events, 5.5 us)
Async XLA Ops:
  0.6 27.7 %copy-start = (bf16[128,64]{0,1:T(8,128)(2,1)S(1)}, bf16[128,64]{0,1:T(8,128)(2,1)}, u32[]{:S(2)}) copy-start(bf16[128,64]{0,1:T(8,128)(2,1)} %param.12) | copy-start | bytes 49156
  0.6 4.6 %copy-start.1 = (bf16[128,1024]{1,0:T(8,128)(2,1)S(1)}, bf16[128,1024]{1,0:T(8,128)(2,1)}, u32[]{:S(2)}) copy-start(bf16[128,1024]{1,0:T(8,128)(2,1)} %param.8) | copy-start | bytes 786436
  0.7 4.7 %copy-start.2 = (bf16[128,64]{0,1:T(8,128)(2,1)S(1)}, bf16[128,64]{0,1:T(8,128)(2,1)}, u32[]{:S(2)}) copy-start(bf16[128,64]{0,1:T(8,128)(2,1)} %param.13) | copy-start | bytes 49156
  6.6 63.5 %all-to-all-start = ((bf16[64,49,128]{2,1,0:T(8,128)(2,1)}), bf16[64,49,128]{2,1,0:T(8,128)(2,1)S(1)}, u32[]{:S(2)}, u32[]{:S(2)}) async-start(bf16[64,49,128]{2,1,0:T(8,128)(2,1)} %pad_maximum_fusion), calls=%async_computation | async-start | bytes 1835008 | tf_op jit(solution)/shard_map/all_to_all | solution.py:231
where the time goes:
time: 179 us
  blocking collectives  78.7 us (44%)
  waiting for transfers between devices  39.9 us (22%)
  starting transfers between devices  21.7 us (12%)
  other arithmetic  11.5 us (6%)
  local copies, waits for them, and re-layouts  11 us (6%)
  matrix products  10.1 us (6%)
  between operations  5.51 us (3%)
    all_to_all x1, blocking collectives, body(): back = lax.all_to_all(returned, 'ctx', 0, 0, tiled=True)  57.7 us
    all_to_all x1, waiting for transfers between devices, body(): arrived = lax.all_to_all(outbound, 'ctx', 0, 0, tiled=True)  39.9 us
    all_to_all x1, starting transfers between devices, body(): arrived = lax.all_to_all(outbound, 'ctx', 0, 0, tiled=True)  21.7 us
    psum x1, blocking collectives, channel_work(): squares = lax.psum(squares, 'ch')  21 us
    unnamed x22, local copies, waits for them, and re-layouts  8.99 us
  transfers between devices with their start and end apart: 1, of which 1 were waited for; matrix products, arithmetic and copies ran while one was open for 1% of the time, Pallas kernels for 0%

commit v1 on v0

--- a/solution.py
+++ b/solution.py
@@ -185,7 +185,7 @@
         * scale
     )
     squares = jnp.sum(jnp.square(lagged.astype(wide_type))) + jnp.sum(grad_medium * grad_medium)
-    squares = lax.psum(squares, "ch")
+    squares = jnp.sum(lax.all_gather(squares, "ch"), axis=0)
     medium_high, medium_low = split_wide(grad_medium)
     squares_high, squares_low = split_wide(squares)
     squares_row = jnp.concatenate(

time: 179 us -> 180 us (level)
  local copies, waits for them, and re-layouts: 11 us -> 13.1 us
    psum x1 -> x0, blocking collectives: 21 us -> none  [channel_work(): squares = lax.psum(squares, 'ch')]
    unnamed x0 -> x1, blocking collectives: none -> 20.5 us
    unnamed x22 -> x25, local copies, waits for them, and re-layouts: 8.99 us -> 11 us
  transfers between devices with their start and end apart: 1 -> 1, of which waited for: 1 -> 1; matrix products, arithmetic and copies ran while one was open for 1% -> 2% of each run, Pallas kernels for 0% -> 0%
where the time goes in v1:
time: 180 us; the launch traced here: 179 us
  blocking collectives  78.2 us (43%)
  waiting for transfers between devices  38.6 us (21%)
  starting transfers between devices  21.7 us (12%)
  local copies, waits for them, and re-layouts  13.1 us (7%)
  other arithmetic  12.1 us (7%)
  matrix products  10.1 us (6%)
  between operations  5.53 us (3%)
    all_to_all x1, blocking collectives, body(): back = lax.all_to_all(returned, 'ctx', 0, 0, tiled=True)  57.7 us
    all_to_all x1, waiting for transfers between devices, body(): arrived = lax.all_to_all(outbound, 'ctx', 0, 0, tiled=True)  38.6 us
    all_to_all x1, starting transfers between devices, body(): arrived = lax.all_to_all(outbound, 'ctx', 0, 0, tiled=True)  21.7 us
    unnamed x1, blocking collectives  20.5 us
    unnamed x25, local copies, waits for them, and re-layouts  11 us
  transfers between devices with their start and end apart: 1, of which 1 were waited for; matrix products, arithmetic and copies ran while one was open for 2% of the time, Pallas kernels for 0%

profile of v1, /device:TPU:1, one launch (start us, length us, event | category | flops | bytes accessed | tf_op | source)
XLA Modules:
  0.0 179.3 jit_solution(17139576095074549434)
XLA Ops:
  0.7 1.2 copy.100
  1.8 1.1 copy.99
  3.0 1.1 copy.101
  4.1 1.1 copy.102
  5.6 1.0 pad_maximum_fusion
  6.6 21.7 %all-to-all-start = ((bf16[64,49,128]{2,1,0:T(8,128)(2,1)}), bf16[64,49,128]{2,1,0:T(8,128)(2,1)S(1)}, u32[]{:S(2)}, u32[]{:S(2)}) async-start(bf16[64,49,128]{2,1,0:T(8,128)(2,1)} %pad_maximum_fusion), calls=%async_computation | async-start | bytes 1835008 | tf_op jit(solution)/shard_map/all_to_all | solution.py:231
  28.6 0.4 slice_reduce_fusion
  28.9 0.3 reshape.489
  29.2 1.3 dynamic-slice
  31.5 38.6 %all-to-all-done = bf16[64,49,128]{2,1,0:T(8,128)(2,1)S(1)} async-done(((bf16[64,49,128]{2,1,0:T(8,128)(2,1)}), bf16[64,49,128]{2,1,0:T(8,128)(2,1)S(1)}, u32[]{:S(2)}, u32[]{:S(2)}) %all-to-all-start) | async-done | bytes 802848 | tf_op jit(solution)/shard_map/all_to_all | solution.py:231
  70.9 1.3 convolution_bitcast_fusion
  72.2 0.8 multiply_add_fusion.1
  73.1 2.1 %fusion.12 = f32[32,2,128,128]{2,3,0,1:T(8,128)S(1)} fusion(f32[32,1,128,128]{2,3,1,0:T(8,128)S(1)} %get-tuple-element.38, f32[32,1,128,128]{2,3,1,0:T(8,128)S(1)} %get-tuple-element.37, f32[1,2,128,128]{2,3,0,1:T(8,128)S(1)} %get-tuple-element.64, f32[1,2,128,128]{2,3,0,1:T(8,128)S(1)} %get-tuple-element.71), kind=kOutput, calls=%fused_computation.16 | convolution fusion | flops 1611726848 | bytes 8650752 | tf_op jit(solution)/shard_map/mkab,kjbq->mjaq/dot_general | solution.py:58
  76.3 1.2 multiply_add_fusion.2
  77.8 2.1 %fusion.9 = f32[32,2,128,128]{2,3,1,0:T(8,128)S(1)} fusion(f32[16,2,128,128]{2,3,0,1:T(8,128)S(1)} %maximum_bitcast_fusion.6, f32[16,2,128,128]{2,3,0,1:T(8,128)S(1)} %maximum_bitcast_fusion.5, f32[1,2,128,128]{2,3,1,0:T(8,128)S(1)} %get-tuple-element.72, f32[1,2,128,128]{2,3,1,0:T(8,128)S(1)} %get-tuple-element.63), kind=kOutput, calls=%fused_computation.15 | convolution fusion | flops 1611726848 | bytes 8650752 | tf_op jit(solution)/shard_map/mkab,kjbq->mjaq/dot_general | solution.py:63
  79.9 0.8 multiply_subtract_fusion
  80.7 2.2 %fusion.19 = bf16[64,32,128]{2,0,1:T(8,128)(2,1)S(1)} fusion(f32[32,1,128,128]{2,3,1,0:T(8,128)S(1)} %get-tuple-element.36, f32[32,1,128,128]{2,3,1,0:T(8,128)S(1)} %get-tuple-element.35, f32[1,64,128]{2,1,0:T(8,128)S(1)} %get-tuple-element.79, f32[1,64,128]{2,1,0:T(8,128)S(1)} %get-tuple-element.80), kind=kOutput, calls=%fused_computation.29 | convolution fusion | flops 404242432 | bytes 4784128 | tf_op jit(solution)/shard_map/kna,mkab->nmb/dot_general | solution.py:73
  83.9 2.5 %add_reduce_fusion = f32[128]{0:T(128)S(1)} fusion(f32[128,128]{1,0:T(8,128)S(1)} %convolution_bitcast_fusion.4, f32[128,128]{1,0:T(8,128)S(1)} %convolution_bitcast_fusion.5), kind=kLoop, calls=%fused_computation | loop fusion | flops 16777088 | bytes 131584 | tf_op jit(solution)/shard_map/reduce_sum | solution.py:181
  86.4 0.6 bitcast_convert_fusion
  88.2 0.6 multiply_reduce_fusion
  90.2 0.8 dynamic-update-slice
  90.9 20.5 %all-reduce.4 = f32[8]{0:T(128)S(1)} all-reduce(f32[8]{0:T(128)S(1)} %dynamic-update-slice), channel_id=1, replica_groups=mesh['ctx'=64,'ch'=8] {'ch'}, use_global_device_ids=true, to_apply=%add.4 | all-reduce | flops 8 | bytes 64
  111.4 0.6 reduce_sum.58
  113.4 0.6 copy.118
  114.0 57.7 %all_to_all.10 = bf16[64,52,128]{2,1,0:T(8,128)(2,1)S(1)} all-to-all(bf16[64,52,128]{2,1,0:T(8,128)(2,1)S(1)} %copy.118), channel_id=1, replica_groups=mesh['ctx'=64,'ch'=8] {'ctx'}, dimensions={0} | all-to-all | bytes 1703936 | tf_op jit(solution)/shard_map/all_to_all | solution.py:244
  172.0 0.8 copy.121
  172.9 0.8 copy.124
  173.8 0.8 copy.123
  174.6 0.8 copy.122
  175.6 0.7 add_reduce_fusion.1
  176.9 0.6 copy.173
  177.5 0.7 fusion.83
  (56 shorter events, 6.3 us)
Async XLA Ops:
  0.6 27.7 %copy-start = (bf16[128,64]{0,1:T(8,128)(2,1)S(1)}, bf16[128,64]{0,1:T(8,128)(2,1)}, u32[]{:S(2)}) copy-start(bf16[128,64]{0,1:T(8,128)(2,1)} %param.12) | copy-start | bytes 49156
  0.6 4.6 %copy-start.1 = (bf16[128,1024]{1,0:T(8,128)(2,1)S(1)}, bf16[128,1024]{1,0:T(8,128)(2,1)}, u32[]{:S(2)}) copy-start(bf16[128,1024]{1,0:T(8,128)(2,1)} %param.8) | copy-start | bytes 786436
  0.7 4.7 %copy-start.2 = (bf16[128,64]{0,1:T(8,128)(2,1)S(1)}, bf16[128,64]{0,1:T(8,128)(2,1)}, u32[]{:S(2)}) copy-start(bf16[128,64]{0,1:T(8,128)(2,1)} %param.13) | copy-start | bytes 49156
  6.6 63.5 %all-to-all-start = ((bf16[64,49,128]{2,1,0:T(8,128)(2,1)}), bf16[64,49,128]{2,1,0:T(8,128)(2,1)S(1)}, u32[]{:S(2)}, u32[]{:S(2)}) async-start(bf16[64,49,128]{2,1,0:T(8,128)(2,1)} %pad_maximum_fusion), calls=%async_computation | async-start | bytes 1835008 | tf_op jit(solution)/shard_map/all_to_all | solution.py:231
